TPU v7x, 32 devices: a whole 2x2x4 slice. The times are simulated.
32 devices in a mesh: dp: 4 (over y, x), seq: 8 (over z, core).
Axes of the slice: x: 2, y: 2, z: 4, core: 2. Of those that a mesh axis runs over, the one named last changes fastest.
Arguments:
- asking_vectors_matrix: bfloat16 [4, 1024, 2048], P('dp', 'seq'), may hold values from -6 to 6
- matched_keys_matrix: bfloat16 [4, 1024, 2048], P('dp', 'seq'), may hold values from -6 to 6
- carried_vectors_matrix: bfloat16 [4, 1024, 2048], P('dp', 'seq'), may hold values from -6 to 6
- upstream_cotangent: bfloat16 [4, 1024, 2048], P('dp', 'seq'), may hold values from -6 to 6
- w_out: bfloat16 [2048, 2048], P('seq'), may hold values from -0.125 to 0.125
- panel_entry_offsets: int32 [4, 9], P('dp'), may hold values from 0 to 32, as said below
- rightward_panel_per_entry: int32 [4, 32], P('dp'), may hold values from 0 to 7, as said below
Outputs:
- layer_out: bfloat16 [4, 1024, 2048], P('dp', 'seq')
- q_grad: bfloat16 [4, 1024, 2048], P('dp', 'seq')
- k_grad: bfloat16 [4, 1024, 2048], P('dp', 'seq')
- v_grad: bfloat16 [4, 1024, 2048], P('dp', 'seq')
- w_out_grad: float32 [2048, 2048], P('seq')
Inputs may be any that keep to these rules, and one draw needn't show every extreme that they name: panel_entry_offsets[b, 0] is 0 and panel_entry_offsets never falls along a row; tile row r owns slots panel_entry_offsets[b, r] to panel_entry_offsets[b, r + 1] - 1, 1 to 8 of them, and its own tile r is among its blocks; in every subgraph one tile row holds all 8 tiles; panel_entry_offsets[b, 8], the used slots, lies between 16 and 32 and equals 32 for at least one subgraph. `rightward_panel_per_entry`: the slots of a tile row hold distinct column tiles in rising order; slots from panel_entry_offsets[b, 8] on hold arbitrary tile numbers that take no part.
All inputs are finite; a program needn't handle non-finite values.
Results may differ from a plain program's by a relative error of at most 0.034.
Values may be sent and summed in bfloat16 or wider, within the bound.
No kernel may reach another device: no remote copies, remote signals or barrier semaphores. Data moves between devices by JAX's collectives and lax.ppermute only.
A program may use at most 128 MiB of HBM per device.

v0:
```python
import math
import jax
import jax.numpy as jnp
from jax import lax
from jax.sharding import PartitionSpec as P

H = 16
HD = 128


def tile_mask(starts, columns, nodes):
    tile_count = starts.shape[0] - 1
    slot_count = columns.shape[0]
    tile_size = nodes // tile_count
    slot_index = jnp.arange(slot_count, dtype=jnp.int32)
    entry_row = jnp.sum((starts[1:][None, :] <= slot_index[:, None]).astype(jnp.int32), axis=1)
    tile_ids = jnp.arange(tile_count, dtype=jnp.int32)
    row_hot = (entry_row[:, None] == tile_ids[None, :]).astype(jnp.int32)
    col_hot = (columns[:, None] == tile_ids[None, :]).astype(jnp.int32)
    pairs = jnp.einsum("er,ec->rc", row_hot, col_hot) > 0
    full = jnp.broadcast_to(pairs[:, None, :, None], (tile_count, tile_size, tile_count, tile_size))
    return jnp.where(full.reshape(nodes, nodes), 0.0, -jnp.inf)


def attend(q, k, v, allowed):
    factor = 1.0 / math.sqrt(q.shape[-1])
    scores = jnp.dot(q, k.T, preferred_element_type=jnp.float32) * factor
    masked = scores + allowed
    row_max = jnp.max(masked, axis=1, keepdims=True)
    expd = jnp.exp(masked - row_max)
    row_total = jnp.sum(expd, axis=1, keepdims=True)
    weighted = jnp.dot(expd.astype(jnp.bfloat16), v, preferred_element_type=jnp.float32)
    attended = (weighted / row_total).astype(jnp.bfloat16)
    return (attended, expd, row_total)


def attend_back(q, k, v, g, attended, expd, row_total):
    factor = 1.0 / math.sqrt(q.shape[-1])
    prob = expd * (1.0 / row_total)
    prob_low = prob.astype(jnp.bfloat16)
    v_grad = jnp.dot(prob_low.T, g, preferred_element_type=jnp.float32)
    prob_grad = jnp.dot(g, v.T, preferred_element_type=jnp.float32)
    delta = jnp.sum(attended.astype(jnp.float32) * g.astype(jnp.float32), axis=1, keepdims=True)
    score_grad = (prob * (prob_grad - delta) * factor).astype(jnp.bfloat16)
    q_grad = jnp.dot(score_grad, k, preferred_element_type=jnp.float32)
    k_grad = jnp.dot(score_grad.T, q, preferred_element_type=jnp.float32)
    return (q_grad.astype(jnp.bfloat16), k_grad.astype(jnp.bfloat16), v_grad.astype(jnp.bfloat16))


def chip_layer_out(att_flat, w_out):
    n = lax.axis_size("seq")
    rows = att_flat.shape[0] // n
    chips = n // 2
    s = lax.axis_index("seq")
    core = s % 2
    z = s // 2
    sibling = [(i, i ^ 1) for i in range(n)]
    att_sib = lax.ppermute(att_flat, "seq", sibling)
    w_sib = lax.ppermute(w_out, "seq", sibling)

    def parity_rows(values):
        quads = values.reshape(chips, 2, rows, values.shape[1])
        return jnp.where(core == 0, quads[:, 0], quads[:, 1])

    att_chip = jnp.concatenate([parity_rows(att_flat), parity_rows(att_sib)], axis=2)
    w_chip = jnp.concatenate([w_out, w_sib], axis=0)
    chip_partial = lax.dot_general(
        att_chip, w_chip, (((2,), (0,)), ((), ())), preferred_element_type=jnp.float32
    )
    total = lax.dynamic_index_in_dim(chip_partial, z, 0, keepdims=False)
    sent = chip_partial.astype(jnp.bfloat16)
    for k in range(1, chips):
        pairs = [(i, (i // 2 + k) % chips * 2 + i % 2) for i in range(n)]
        piece = lax.dynamic_index_in_dim(sent, (z + k) % chips, 0, keepdims=False)
        total = total + lax.ppermute(piece, "seq", pairs).astype(jnp.float32)
    return total


def shards(
    asking_vectors_matrix,
    matched_keys_matrix,
    carried_vectors_matrix,
    upstream_cotangent,
    w_out,
    panel_entry_offsets,
    rightward_panel_per_entry,
):
    nodes_here = asking_vectors_matrix.shape[1]
    width = asking_vectors_matrix.shape[2]
    n_seq = lax.axis_size("seq")
    nodes = nodes_here * n_seq
    grad_here = upstream_cotangent[0]
    grad_full = lax.all_gather(grad_here, "seq", axis=0, tiled=True)
    groups = n_seq
    group_width = width // groups
    local_heads = group_width // HD

    def to_groups(values):
        return values.reshape(nodes_here, groups, group_width).transpose(1, 0, 2)

    stacked = jnp.stack(
        [
            to_groups(asking_vectors_matrix[0]),
            to_groups(matched_keys_matrix[0]),
            to_groups(carried_vectors_matrix[0]),
        ]
    )
    heads = lax.all_to_all(stacked, "seq", split_axis=1, concat_axis=1, tiled=True)
    heads = heads.reshape(3, nodes, group_width)
    allowed = tile_mask(panel_entry_offsets[0], rightward_panel_per_entry[0], nodes)

    def head_cols(values, h):
        return values[:, h * HD : (h + 1) * HD]

    fwd = [
        attend(head_cols(heads[0], h), head_cols(heads[1], h), head_cols(heads[2], h), allowed)
        for h in range(local_heads)
    ]
    att_flat = jnp.concatenate([f[0] for f in fwd], axis=1)
    layer_out = chip_layer_out(att_flat, w_out).astype(jnp.bfloat16)[None]
    g_flat = lax.dot_general(
        grad_full, w_out, (((1,), (1,)), ((), ())), preferred_element_type=jnp.float32
    ).astype(jnp.bfloat16)
    att_blocks = att_flat.reshape(n_seq, nodes_here, local_heads * HD)
    grad_blocks = grad_full.reshape(n_seq, nodes_here, width)
    terms = jnp.einsum(
        "bnf,bnk->bfk", att_blocks, grad_blocks, preferred_element_type=jnp.float32
    ).astype(jnp.bfloat16)
    w_rows = jnp.sum(terms.astype(jnp.float32), axis=0)
    w_rows = lax.psum(w_rows.astype(jnp.bfloat16), "dp").astype(jnp.float32)
    batch = asking_vectors_matrix.shape[0] * lax.axis_size("dp")
    w_out_grad = w_rows / batch
    bwd = [
        attend_back(
            head_cols(heads[0], h),
            head_cols(heads[1], h),
            head_cols(heads[2], h),
            head_cols(g_flat, h),
            fwd[h][0],
            fwd[h][1],
            fwd[h][2],
        )
        for h in range(local_heads)
    ]
    grads = jnp.stack(
        [
            jnp.concatenate([b[i] for b in bwd], axis=1).reshape(groups, nodes_here, group_width)
            for i in range(3)
        ]
    )
    back = lax.all_to_all(grads, "seq", split_axis=1, concat_axis=1, tiled=True)
    back = back.transpose(0, 2, 1, 3).reshape(3, 1, nodes_here, width)
    return (layer_out, back[0], back[1], back[2], w_out_grad)


def solution(mesh):
    return jax.shard_map(
        shards,
        mesh=mesh,
        in_specs=(
            P("dp", "seq", None),
            P("dp", "seq", None),
            P("dp", "seq", None),
            P("dp", "seq", None),
            P("seq", None),
            P("dp", None),
            P("dp", None),
        ),
        out_specs=(
            P("dp", "seq", None),
            P("dp", "seq", None),
            P("dp", "seq", None),
            P("dp", "seq", None),
            P("seq", None),
        ),
        check_vma=False,
    )
```

profile of v0, /device:TPU:10, one launch (start us, length us, event | category | flops | bytes accessed | tf_op | source)
XLA Modules:
  0.0 211.3 jit_solution(6985377320653367382)
XLA Ops:
  7.2 0.7 all-gather.3.cloned.1.call-update
  7.9 1.3 copy.72
  9.2 1.3 copy.73
  10.5 1.3 copy.74
  11.9 0.2 pad_maximum_fusion
  12.1 1.2 copy.75
  13.3 5.3 %all-to-all-start = ((bf16[3,8,128,256]{2,3,0,1:T(8,128)(2,1)}), bf16[3,8,128,256]{2,3,0,1:T(8,128)(2,1)S(1)}, u32[]{:S(2)}, u32[]{:S(2)}) async-start(bf16[3,8,128,256]{2,3,0,1:T(8,128)(2,1)} %copy.75), calls=%async_computation | async-start | bytes 3145728 | tf_op jit(solution)/shard_map/all_to_all | solution.py:108
  18.6 0.1 collective-permute-start.1
  18.9 0.1 convert_reduce_fusion.1
  19.0 0.3 fusion.38
  19.3 67.4 %all-to-all-done = bf16[3,8,128,256]{2,3,0,1:T(8,128)(2,1)S(1)} async-done(((bf16[3,8,128,256]{2,3,0,1:T(8,128)(2,1)}), bf16[3,8,128,256]{2,3,0,1:T(8,128)(2,1)S(1)}, u32[]{:S(2)}, u32[]{:S(2)}) %all-to-all-start) | async-done | bytes 1572896 | tf_op jit(solution)/shard_map/all_to_all | solution.py:108
  86.7 0.1 fusion.69
  86.8 0.2 copy.96
  87.1 0.2 copy.95
  87.3 0.2 copy.97
  87.5 0.3 broadcast_in_dim.14
  87.9 1.2 fusion.73
  89.1 0.6 fusion.2
  89.7 1.2 fusion.72
  90.9 0.1 copy-done
  91.1 0.6 fusion.4
  91.7 1.3 copy-done.2
  93.0 0.8 fusion.32
  93.9 3.9 %fusion.21 = bf16[1024,256]{0,1:T(8,128)(2,1)S(1)} fusion(bf16[256,2048]{1,0:T(8,128)(2,1)} %param.11, bf16[1,1024,2048]{2,1,0:T(8,128)(2,1)} %all-gather.3.cloned.1.call-done), kind=kOutput, calls=%fused_computation.32 | convolution fusion | flops 1074003968 | bytes 5767168 | tf_op jit(solution)/shard_map/dot_general | solution.py:121
  97.8 0.9 multiply_reduce_fusion.1
  98.7 1.2 multiply_convert_fusion.1
  99.9 0.5 convolution_convert_fusion.3
  100.4 0.8 convolution_convert_fusion.1
  101.2 0.8 copy-done.3
  102.1 1.2 multiply_convert_fusion
  103.3 0.5 convolution_convert_fusion.2
  103.8 0.8 convolution_convert_fusion
  104.6 1.1 fusion.31
  105.7 0.9 fusion.30
  106.7 1.0 fusion.67
  107.7 0.4 reshape.63
  108.1 0.1 copy.104
  108.4 0.1 copy.105
  108.6 0.1 copy.106
  108.8 1.4 pad_maximum_fusion.1
  110.1 6.9 %all-to-all-start.1 = ((bf16[3,8,128,256]{2,3,0,1:T(8,128)(2,1)}), bf16[3,8,128,256]{2,3,0,1:T(8,128)(2,1)S(1)}, u32[]{:S(2)}, u32[]{:S(2)}) async-start(bf16[3,8,128,256]{2,3,0,1:T(8,128)(2,1)} %pad_maximum_fusion.1), calls=%async_computation.1 | async-start | bytes 3145728 | tf_op jit(solution)/shard_map/all_to_all | solution.py:151
  117.0 1.5 fusion.70
  118.5 1.2 copy.98
  119.8 1.1 copy.99
  120.9 5.9 %convert_reduce_fusion = bf16[256,2048]{1,0:T(8,128)(2,1)} fusion(bf16[8,128,2048]{2,1,0:T(8,128)(2,1)} %bitcast.122, bf16[32,8,8,128]{3,2,1,0:T(8,128)(2,1)} %get-tuple-element.26), kind=kOutput, calls=%fused_computation | convolution fusion | flops 1081606144 | bytes 5767168 | tf_op jit(solution)/shard_map/bnf,bnk->bfk/dot_general | solution.py:126
  126.8 1.4 reshape.64
  128.2 0.7 fusion.71
  128.9 0.5 copy.100
  129.4 0.5 copy.101
  130.0 4.7 %fusion.74 = (bf16[4,128,2048]{2,1,0:T(8,128)(2,1)S(1)}, f32[4,128,2048]{2,1,0:T(8,128)}) fusion(bf16[256,2048]{1,0:T(8,128)(2,1)} %collective-permute-done.1, bf16[256,2048]{1,0:T(8,128)(2,1)} %param.11, bf16[4,128,256]{2,1,0:T(8,128)(2,1)S(1)} %get-tuple-element.39, bf16[4,128,256]{2,1,0:T(8,128)(2,1)S(1)} %get-tuple-element.40), kind=kOutput, calls=%fused_computation.99 | convolution fusion | flops 1080033280 | bytes 8912896 | tf_op jit(solution)/shard_map/dot_general | solution.py:67
  134.7 0.2 dynamic-slice_bitcast_fusion.2
  134.9 1.5 collective-permute-start.2
  136.4 1.0 collective-permute-start.3
  137.5 1.9 collective-permute-start.4
  139.4 41.1 %all-reduce.2.cloned.1.call-done = bf16[256,2048]{1,0:T(8,128)(2,1)} async-done(((bf16[256,2048]{1,0:T(8,128)(2,1)}), bf16[256,2048]{1,0:T(8,128)(2,1)}) %all-reduce.2.cloned.1.call-update) | async-done | bytes 1048592 | tf_op jit(solution)/shard_map/psum | solution.py:130
  180.4 2.8 %convert_multiply_fusion = f32[256,2048]{1,0:T(8,128)} fusion(bf16[256,2048]{1,0:T(8,128)(2,1)} %all-reduce.2.cloned.1.call-done), kind=kLoop, calls=%fused_computation.23 | loop fusion | flops 1048576 | bytes 3145728 | tf_op jit(solution)/shard_map/div | solution.py:132
  183.2 1.9 collective-permute-done.2
  185.1 11.2 %collective-permute-done.3 = bf16[128,2048]{1,0:T(8,128)(2,1)} collective-permute-done((bf16[128,2048]{1,0:T(8,128)(2,1)S(1)}, bf16[128,2048]{1,0:T(8,128)(2,1)}, u32[]{:S(2)}, u32[]{:S(2)}) %collective-permute-start.3) | collective-permute-done | bytes 524320 | tf_op jit(solution)/shard_map/ppermute | solution.py:75
  196.3 2.2 %collective-permute-done.4 = bf16[128,2048]{1,0:T(8,128)(2,1)} collective-permute-done((bf16[128,2048]{1,0:T(8,128)(2,1)S(1)}, bf16[128,2048]{1,0:T(8,128)(2,1)}, u32[]{:S(2)}, u32[]{:S(2)}) %collective-permute-start.4) | collective-permute-done | bytes 524320 | tf_op jit(solution)/shard_map/ppermute | solution.py:75
  198.5 2.8 %fusion.42 = bf16[1,128,2048]{2,1,0:T(8,128)(2,1)} fusion(bf16[128,2048]{1,0:T(8,128)(2,1)} %collective-permute-done.4, bf16[128,2048]{1,0:T(8,128)(2,1)} %collective-permute-done.3, bf16[128,2048]{1,0:T(8,128)(2,1)} %collective-permute-done.2, f32[4,128,2048]{2,1,0:T(8,128)} %get-tuple-element.37, s32[]{:T(128)S(6)} %select_n.72), kind=kLoop, calls=%fused_computation.49 | loop fusion | flops 1835008 | bytes 3145732 | tf_op jit(solution)/shard_map/broadcast_in_dim | solution.py:120
  201.3 0.1 fusion.68
  201.4 1.0 copy.90
  202.4 1.0 copy.91
  203.4 1.0 copy.92
  (28 shorter events, 0.7 us)
Async XLA Ops:
  7.2 86.7 %all-gather.3.cloned.1.call-start = ((), (), s32[]{:S(2)}) async-start(), calls=%async_computation.3 | async-start | bytes 4718592 | tf_op jit(solution)/shard_map/all_gather | solution.py:93
  11.9 6.9 %copy-start.4 = (s32[1,9]{1,0:T(1,128)S(1)}, s32[1,9]{1,0:T(1,128)}, u32[]{:S(2)}) copy-start(s32[1,9]{1,0:T(1,128)} %param.12) | copy-start | bytes 112
  11.9 7.1 %copy-start.5 = (s32[1,32]{1,0:T(1,128)S(1)}, s32[1,32]{1,0:T(1,128)}, u32[]{:S(2)}) copy-start(s32[1,32]{1,0:T(1,128)} %param.13) | copy-start | bytes 388
  13.3 73.4 %all-to-all-start = ((bf16[3,8,128,256]{2,3,0,1:T(8,128)(2,1)}), bf16[3,8,128,256]{2,3,0,1:T(8,128)(2,1)S(1)}, u32[]{:S(2)}, u32[]{:S(2)}) async-start(bf16[3,8,128,256]{2,3,0,1:T(8,128)(2,1)} %copy.75), calls=%async_computation | async-start | bytes 3145728 | tf_op jit(solution)/shard_map/all_to_all | solution.py:108
  18.6 111.3 %collective-permute-start.1 = (bf16[256,2048]{1,0:T(8,128)(2,1)}, bf16[256,2048]{1,0:T(8,128)(2,1)}, u32[]{:S(2)}, u32[]{:S(2)}) collective-permute-start(bf16[256,2048]{1,0:T(8,128)(2,1)} %param.11), channel_id=1, source_target_pairs={{0,1},{1,0},{2,3},{3,2},{4,5},{5,4},{6,7},{7,6},{8,9},{9,8},{10,11... | collective-permute-start | bytes 3145736 | tf_op jit(solution)/shard_map/ppermute | solution.py:59
  89.1 2.0 copy-start
  91.1 2.0 copy-start.2
  93.9 3.9 %copy-start.1 = (f32[1024,1024]{0,1:T(8,128)S(1)}, f32[1024,1024]{0,1:T(8,128)}, u32[]{:S(2)}) copy-start(f32[1024,1024]{0,1:T(8,128)} %copy-done) | copy-start | bytes 12582916
  99.9 2.2 %copy-start.3 = (f32[1024,1024]{0,1:T(8,128)S(1)}, f32[1024,1024]{0,1:T(8,128)}, u32[]{:S(2)}) copy-start(f32[1024,1024]{0,1:T(8,128)} %copy-done.2) | copy-start | bytes 12582916
  107.6 19.1 %collective-permute-start = (bf16[1024,256]{0,1:T(8,128)(2,1)S(1)}, bf16[1024,256]{0,1:T(8,128)(2,1)}, u32[]{:S(2)}, u32[]{:S(2)}) collective-permute-start(bf16[1024,256]{0,1:T(8,128)(2,1)S(1)} %get-tuple-element.27), channel_id=1, source_target_pairs={{0,1},{1,0},{2,3},{3,2},{4,5},{5,4},{6,7},{7,6},{8,9},{9,8},{10,11... | collective-permute-start | bytes 1572872 | tf_op jit(solution)/shard_map/ppermute | solution.py:58
  110.1 91.2 %all-to-all-start.1 = ((bf16[3,8,128,256]{2,3,0,1:T(8,128)(2,1)}), bf16[3,8,128,256]{2,3,0,1:T(8,128)(2,1)S(1)}, u32[]{:S(2)}, u32[]{:S(2)}) async-start(bf16[3,8,128,256]{2,3,0,1:T(8,128)(2,1)} %pad_maximum_fusion.1), calls=%async_computation.1 | async-start | bytes 3145728 | tf_op jit(solution)/shard_map/all_to_all | solution.py:151
  117.0 63.4 %all-reduce.2.cloned.1.call-start = ((), (), s32[]{:S(2)}) async-start(), calls=%async_computation.2 | async-start | bytes 2097152 | tf_op jit(solution)/shard_map/psum | solution.py:130
  134.9 50.2 %collective-permute-start.2 = (bf16[128,2048]{1,0:T(8,128)(2,1)S(1)}, bf16[128,2048]{1,0:T(8,128)(2,1)}, u32[]{:S(2)}, u32[]{:S(2)}) collective-permute-start(bf16[128,2048]{1,0:T(8,128)(2,1)S(1)} %get-tuple-element.17), channel_id=1, source_target_pairs={{0,2},{1,3},{2,4},{3,5},{4,6},{5,7},{6,0},{7,1},{8,10},{9,11},{10,... | collective-permute-start | bytes 1572872 | tf_op jit(solution)/shard_map/ppermute | solution.py:75
  136.4 59.8 %collective-permute-start.3 = (bf16[128,2048]{1,0:T(8,128)(2,1)S(1)}, bf16[128,2048]{1,0:T(8,128)(2,1)}, u32[]{:S(2)}, u32[]{:S(2)}) collective-permute-start(bf16[128,2048]{1,0:T(8,128)(2,1)S(1)} %get-tuple-element.19), channel_id=1, source_target_pairs={{0,4},{1,5},{2,6},{3,7},{4,0},{5,1},{6,2},{7,3},{8,12},{9,13},{10,... | collective-permute-start | bytes 1572872 | tf_op jit(solution)/shard_map/ppermute | solution.py:75
  137.5 61.0 %collective-permute-start.4 = (bf16[128,2048]{1,0:T(8,128)(2,1)S(1)}, bf16[128,2048]{1,0:T(8,128)(2,1)}, u32[]{:S(2)}, u32[]{:S(2)}) collective-permute-start(bf16[128,2048]{1,0:T(8,128)(2,1)S(1)} %get-tuple-element.18), channel_id=1, source_target_pairs={{0,6},{1,7},{2,0},{3,1},{4,2},{5,3},{6,4},{7,5},{8,14},{9,15},{10,... | collective-permute-start | bytes 1572872 | tf_op jit(solution)/shard_map/ppermute | solution.py:75
Sparse Core Ops, SparseCore 0:
  9.6 77.0 all-gather.2
  126.9 53.4 all-reduce.1
where the time goes:
time: 212 us; the launch traced here: 211 us
  waiting for transfers between devices  124 us (58%)
  matrix products  25.9 us (12%)
  local copies, waits for them, and re-layouts  19.9 us (9%)
  starting transfers between devices  17 us (8%)
  between operations  14.4 us (7%)
  other arithmetic  9.61 us (5%)
    all_to_all x1, waiting for transfers between devices, shards(): lax.all_to_all(stacked, 'seq', split_axis=1, concat_axis=1, tiled=True)  67.4 us
    psum x1, waiting for transfers between devices, shards(): w_rows = lax.psum(w_rows.astype(jnp.bfloat16), 'dp').astype(jnp.float32)  41.1 us
    ppermute x3, waiting for transfers between devices, chip_layer_out(): total = total + lax.ppermute(piece, 'seq', pairs).astype(jnp.float32)  15.3 us
    unnamed x28, local copies, waits for them, and re-layouts  13.5 us
    all_to_all x1, starting transfers between devices, shards(): back = lax.all_to_all(grads, 'seq', split_axis=1, concat_axis=1, tiled=True)  6.9 us
    dot_general x1, matrix products, shards(): jnp.einsum('bnf,bnk->bfk', att_blocks, grad_blocks, preferred_element_typ...  5.87 us
    all_to_all x1, starting transfers between devices, shards(): lax.all_to_all(stacked, 'seq', split_axis=1, concat_axis=1, tiled=True)  5.32 us
    dot_general x1, matrix products, chip_layer_out(): lax.dot_general(att_chip, w_chip, (((2,), (0,)), ((), ())), preferred_ele...  4.73 us
  transfers between devices with their start and end apart: 9, of which 5 were waited for; matrix products, arithmetic and copies ran while one was open for 24% of the time, Pallas kernels for 0%

commit v1 on v0

--- a/solution.py
+++ b/solution.py
@@ -127,7 +127,7 @@
         "bnf,bnk->bfk", att_blocks, grad_blocks, preferred_element_type=jnp.float32
     ).astype(jnp.bfloat16)
     w_rows = jnp.sum(terms.astype(jnp.float32), axis=0)
-    w_rows = lax.psum(w_rows.astype(jnp.bfloat16), "dp").astype(jnp.float32)
+    w_rows = jnp.sum(lax.all_gather(w_rows.astype(jnp.bfloat16), "dp"), axis=0).astype(jnp.float32)
     batch = asking_vectors_matrix.shape[0] * lax.axis_size("dp")
     w_out_grad = w_rows / batch
     bwd = [

time: 212 us -> 222 us (1.047)
  waiting for transfers between devices: 124 us -> 132 us
    ppermute x3, waiting for transfers between devices: 15.3 us -> 64.1 us  [chip_layer_out(): total = total + lax.ppermute(piece, 'seq', pairs).astype(jnp.float32)]
    psum x1 -> x0, waiting for transfers between devices: 41.1 us -> none  [shards(): w_rows = lax.psum(w_rows.astype(jnp.bfloat16), 'dp').astype(jnp.float32)]
    reduce_sum x0 -> x1, other arithmetic: none -> 3.07 us  [shards(): jnp.sum(lax.all_gather(w_rows.astype(jnp.bfloat16), 'dp'), axis=0)]
    dot_general x1, matrix products: 5.87 us -> 3.41 us  [shards(): jnp.einsum('bnf,bnk->bfk', att_blocks, grad_blocks, preferred_element_typ...]
    dot_general x2, matrix products: 2.39 us -> 4.75 us  [attend_back(): prob_grad = jnp.dot(g, v.T, preferred_element_type=jnp.float32)]
    unnamed x28 -> x32, local copies, waits for them, and re-layouts: 13.5 us -> 14.1 us
  transfers between devices with their start and end apart: 9 -> 9, of which waited for: 5 -> 4; matrix products, arithmetic and copies ran while one was open for 24% -> 19% of each run, Pallas kernels for 0% -> 0%
where the time goes in v1:
time: 222 us
  waiting for transfers between devices  132 us (59%)
  matrix products  25.9 us (12%)
  local copies, waits for them, and re-layouts  20.5 us (9%)
  starting transfers between devices  17.7 us (8%)
  between operations  14.5 us (7%)
  other arithmetic  10.6 us (5%)
    all_to_all x1, waiting for transfers between devices, shards(): lax.all_to_all(stacked, 'seq', split_axis=1, concat_axis=1, tiled=True)  67.6 us
    ppermute x3, waiting for transfers between devices, chip_layer_out(): total = total + lax.ppermute(piece, 'seq', pairs).astype(jnp.float32)  64.1 us
    unnamed x32, local copies, waits for them, and re-layouts  14.1 us
    all_to_all x1, starting transfers between devices, shards(): back = lax.all_to_all(grads, 'seq', split_axis=1, concat_axis=1, tiled=True)  7.36 us
    all_to_all x1, starting transfers between devices, shards(): lax.all_to_all(stacked, 'seq', split_axis=1, concat_axis=1, tiled=True)  5.32 us
    dot_general x1, matrix products, chip_layer_out(): lax.dot_general(att_chip, w_chip, (((2,), (0,)), ((), ())), preferred_ele...  4.79 us
    dot_general x2, matrix products, attend_back(): prob_grad = jnp.dot(g, v.T, preferred_element_type=jnp.float32)  4.75 us
    ppermute x3, starting transfers between devices, chip_layer_out(): total = total + lax.ppermute(piece, 'seq', pairs).astype(jnp.float32)  4.47 us
  transfers between devices with their start and end apart: 9, of which 4 were waited for; matrix products, arithmetic and copies ran while one was open for 19% of the time, Pallas kernels for 0%

profile of v1, /device:TPU:10, one launch (start us, length us, event | category | flops | bytes accessed | tf_op | source)
XLA Modules:
  0.0 221.5 jit_solution(17956990054674170533)
XLA Ops:
  7.2 0.7 all-gather.5.cloned.1.call-update
  7.9 1.3 copy.72
  9.2 1.3 copy.73
  10.5 1.3 copy.74
  11.9 0.2 pad_maximum_fusion
  12.1 1.2 copy.75
  13.3 5.3 %all-to-all-start = ((bf16[3,8,128,256]{2,3,0,1:T(8,128)(2,1)}), bf16[3,8,128,256]{2,3,0,1:T(8,128)(2,1)S(1)}, u32[]{:S(2)}, u32[]{:S(2)}) async-start(bf16[3,8,128,256]{2,3,0,1:T(8,128)(2,1)} %copy.75), calls=%async_computation | async-start | bytes 3145728 | tf_op jit(solution)/shard_map/all_to_all | solution.py:108
  18.8 0.3 fusion.38
  19.1 67.6 %all-to-all-done = bf16[3,8,128,256]{2,3,0,1:T(8,128)(2,1)S(1)} async-done(((bf16[3,8,128,256]{2,3,0,1:T(8,128)(2,1)}), bf16[3,8,128,256]{2,3,0,1:T(8,128)(2,1)S(1)}, u32[]{:S(2)}, u32[]{:S(2)}) %all-to-all-start) | async-done | bytes 1572896 | tf_op jit(solution)/shard_map/all_to_all | solution.py:108
  86.7 0.1 fusion.69
  86.8 0.2 copy.96
  87.1 0.2 copy.95
  87.3 0.2 copy.97
  87.5 0.3 broadcast_in_dim.14
  87.8 1.2 fusion.73
  89.1 0.6 fusion.2
  89.7 1.2 fusion.72
  90.9 0.1 copy-done
  91.0 0.6 fusion.4
  91.7 1.3 copy-done.3
  93.0 0.8 fusion.32
  93.9 3.9 %fusion.21 = bf16[1024,256]{0,1:T(8,128)(2,1)S(1)} fusion(bf16[256,2048]{1,0:T(8,128)(2,1)} %param.11, bf16[1,1024,2048]{2,1,0:T(8,128)(2,1)} %all-gather.5.cloned.1.call-done), kind=kOutput, calls=%fused_computation.32 | convolution fusion | flops 1074003968 | bytes 5767168 | tf_op jit(solution)/shard_map/dot_general | solution.py:121
  97.8 0.9 multiply_reduce_fusion.1
  98.7 0.1 fusion.67
  98.8 1.2 copy-done.5
  100.0 3.4 %convert_reduce_fusion = bf16[256,2048]{1,0:T(8,128)(2,1)} fusion(bf16[8,128,2048]{2,1,0:T(8,128)(2,1)S(1)} %bitcast.124, bf16[32,8,8,128]{3,2,1,0:T(8,128)(2,1)S(1)} %get-tuple-element.26), kind=kOutput, calls=%fused_computation | convolution fusion | flops 1081606144 | bytes 5767168 | tf_op jit(solution)/shard_map/bnf,bnk->bfk/dot_general | solution.py:126
  103.5 3.5 %multiply_convert_fusion.1 = bf16[1024,1024]{0,1:T(8,128)(2,1)S(1)} fusion(f32[1024,1024]{0,1:T(8,128)} %copy-done, f32[1024]{0:T(1024)S(1)} %get-tuple-element.15, f32[1024]{0:T(1024)S(1)} %broadcast_divide_fusion.1, f32[1024]{0:T(1024)S(1)} %get-tuple-element.34, bf16[1024,256]{1,0:T(8,128)(2,1)S(1)} %bitcast.122, bf16[1024,256]{0,1:T(8,128)(2,1)S(1)} %fusion.21), kind=kOutput, calls=%fused_computation.6 | convolution fusion | flops 274726912 | bytes 6828032 | tf_op jit(solution)/shard_map/dot_general | solution.py:42
  107.0 0.5 convolution_convert_fusion.3
  107.5 1.2 multiply_convert_fusion
  108.7 0.7 convolution_convert_fusion.2
  109.5 0.1 copy.104
  109.7 0.8 convolution_convert_fusion.1
  110.5 0.8 convolution_convert_fusion
  111.4 0.1 copy.105
  111.6 0.3 copy-done.2
  111.8 0.9 fusion.31
  112.8 0.9 fusion.30
  114.0 1.3 pad_maximum_fusion.1
  115.3 7.4 %all-to-all-start.1 = ((bf16[3,8,128,256]{2,3,0,1:T(8,128)(2,1)}), bf16[3,8,128,256]{2,3,0,1:T(8,128)(2,1)S(1)}, u32[]{:S(2)}, u32[]{:S(2)}) async-start(bf16[3,8,128,256]{2,3,0,1:T(8,128)(2,1)} %pad_maximum_fusion.1), calls=%async_computation.1 | async-start | bytes 3145728 | tf_op jit(solution)/shard_map/all_to_all | solution.py:151
  122.6 0.1 collective-permute-start
  122.8 0.4 collective-permute-start.1
  123.1 0.4 reshape.63
  123.5 1.5 fusion.70
  125.0 1.2 copy.98
  126.3 1.1 copy.99
  127.4 1.4 reshape.64
  128.8 0.7 fusion.71
  129.5 0.5 copy.100
  130.0 0.5 copy.101
  130.6 4.8 %fusion.74 = (bf16[4,128,2048]{2,1,0:T(8,128)(2,1)S(1)}, f32[4,128,2048]{2,1,0:T(8,128)}) fusion(bf16[256,2048]{1,0:T(8,128)(2,1)} %collective-permute-done.1, bf16[256,2048]{1,0:T(8,128)(2,1)} %param.11, bf16[4,128,256]{2,1,0:T(8,128)(2,1)S(1)} %get-tuple-element.39, bf16[4,128,256]{2,1,0:T(8,128)(2,1)S(1)} %get-tuple-element.40), kind=kOutput, calls=%fused_computation.99 | convolution fusion | flops 1080033280 | bytes 8912896 | tf_op jit(solution)/shard_map/dot_general | solution.py:67
  135.4 0.1 dynamic-slice_bitcast_fusion.2
  135.5 1.5 collective-permute-start.2
  137.1 1.1 collective-permute-start.3
  138.1 1.9 collective-permute-start.4
  140.0 50.7 %collective-permute-done.2 = bf16[128,2048]{1,0:T(8,128)(2,1)} collective-permute-done((bf16[128,2048]{1,0:T(8,128)(2,1)S(1)}, bf16[128,2048]{1,0:T(8,128)(2,1)}, u32[]{:S(2)}, u32[]{:S(2)}) %collective-permute-start.2) | collective-permute-done | bytes 524320 | tf_op jit(solution)/shard_map/ppermute | solution.py:75
  190.7 11.2 %collective-permute-done.3 = bf16[128,2048]{1,0:T(8,128)(2,1)} collective-permute-done((bf16[128,2048]{1,0:T(8,128)(2,1)S(1)}, bf16[128,2048]{1,0:T(8,128)(2,1)}, u32[]{:S(2)}, u32[]{:S(2)}) %collective-permute-start.3) | collective-permute-done | bytes 524320 | tf_op jit(solution)/shard_map/ppermute | solution.py:75
  201.9 2.2 %collective-permute-done.4 = bf16[128,2048]{1,0:T(8,128)(2,1)} collective-permute-done((bf16[128,2048]{1,0:T(8,128)(2,1)S(1)}, bf16[128,2048]{1,0:T(8,128)(2,1)}, u32[]{:S(2)}, u32[]{:S(2)}) %collective-permute-start.4) | collective-permute-done | bytes 524320 | tf_op jit(solution)/shard_map/ppermute | solution.py:75
  204.1 2.8 %fusion.42 = bf16[1,128,2048]{2,1,0:T(8,128)(2,1)} fusion(bf16[128,2048]{1,0:T(8,128)(2,1)} %collective-permute-done.4, bf16[128,2048]{1,0:T(8,128)(2,1)} %collective-permute-done.3, bf16[128,2048]{1,0:T(8,128)(2,1)} %collective-permute-done.2, f32[4,128,2048]{2,1,0:T(8,128)} %get-tuple-element.37, s32[]{:T(128)S(6)} %select_n.72), kind=kLoop, calls=%fused_computation.49 | loop fusion | flops 1835008 | bytes 3145732 | tf_op jit(solution)/shard_map/broadcast_in_dim | solution.py:120
  206.9 0.1 fusion.68
  207.0 1.0 copy.90
  208.0 1.0 copy.91
  209.0 1.0 copy.92
  210.1 3.1 %reduce_sum.75 = bf16[256,2048]{1,0:T(8,128)(2,1)S(1)} reduce(bf16[4,256,2048]{2,1,0:T(8,128)(2,1)} %bitcast.106, bf16[]{:T(256)} %constant.74.clone.1), dimensions={0}, to_apply=%region_8.9 | reduce | flops 1572864 | bytes 5242882 | tf_op jit(solution)/shard_map/reduce_sum | solution.py:130
  213.1 1.6 convert_multiply_fusion
  (33 shorter events, 0.8 us)
Async XLA Ops:
  7.2 86.7 %all-gather.5.cloned.1.call-start = ((), (), s32[]{:S(2)}) async-start(), calls=%async_computation.2 | async-start | bytes 4718592 | tf_op jit(solution)/shard_map/all_gather | solution.py:93
  11.9 6.8 %copy-start.6 = (s32[1,9]{1,0:T(1,128)S(1)}, s32[1,9]{1,0:T(1,128)}, u32[]{:S(2)}) copy-start(s32[1,9]{1,0:T(1,128)} %param.12) | copy-start | bytes 112
  11.9 6.9 %copy-start.7 = (s32[1,32]{1,0:T(1,128)S(1)}, s32[1,32]{1,0:T(1,128)}, u32[]{:S(2)}) copy-start(s32[1,32]{1,0:T(1,128)} %param.13) | copy-start | bytes 388
  13.3 73.4 %all-to-all-start = ((bf16[3,8,128,256]{2,3,0,1:T(8,128)(2,1)}), bf16[3,8,128,256]{2,3,0,1:T(8,128)(2,1)S(1)}, u32[]{:S(2)}, u32[]{:S(2)}) async-start(bf16[3,8,128,256]{2,3,0,1:T(8,128)(2,1)} %copy.75), calls=%async_computation | async-start | bytes 3145728 | tf_op jit(solution)/shard_map/all_to_all | solution.py:108
  18.6 191.4 %all-gather.7.cloned.1.call-start = ((), (), s32[]{:S(2)}) async-start(), calls=%async_computation.3 | async-start | bytes 5242880 | tf_op jit(solution)/shard_map/all_gather | solution.py:130
  89.1 2.0 copy-start
  91.0 2.0 copy-start.3
  93.9 3.9 %copy-start.1 = (f32[1024,1024]{0,1:T(8,128)S(1)}, f32[1024,1024]{0,1:T(8,128)}, u32[]{:S(2)}) copy-start(f32[1024,1024]{0,1:T(8,128)} %copy-done) | copy-start | bytes 12582916
  97.8 2.2 copy-start.5
  103.4 4.1 %copy-start.4 = (f32[1024,1024]{0,1:T(8,128)S(1)}, f32[1024,1024]{0,1:T(8,128)}, u32[]{:S(2)}) copy-start(f32[1024,1024]{0,1:T(8,128)} %copy-done.3) | copy-start | bytes 12582916
  109.7 2.2 copy-start.2
  115.3 91.6 %all-to-all-start.1 = ((bf16[3,8,128,256]{2,3,0,1:T(8,128)(2,1)}), bf16[3,8,128,256]{2,3,0,1:T(8,128)(2,1)S(1)}, u32[]{:S(2)}, u32[]{:S(2)}) async-start(bf16[3,8,128,256]{2,3,0,1:T(8,128)(2,1)} %pad_maximum_fusion.1), calls=%async_computation.1 | async-start | bytes 3145728 | tf_op jit(solution)/shard_map/all_to_all | solution.py:151
  122.6 4.8 %collective-permute-start = (bf16[1024,256]{0,1:T(8,128)(2,1)S(1)}, bf16[1024,256]{0,1:T(8,128)(2,1)}, u32[]{:S(2)}, u32[]{:S(2)}) collective-permute-start(bf16[1024,256]{0,1:T(8,128)(2,1)S(1)} %get-tuple-element.27), channel_id=1, source_target_pairs={{0,1},{1,0},{2,3},{3,2},{4,5},{5,4},{6,7},{7,6},{8,9},{9,8},{10,11... | collective-permute-start | bytes 1572872 | tf_op jit(solution)/shard_map/ppermute | solution.py:58
  122.8 7.8 %collective-permute-start.1 = (bf16[256,2048]{1,0:T(8,128)(2,1)}, bf16[256,2048]{1,0:T(8,128)(2,1)}, u32[]{:S(2)}, u32[]{:S(2)}) collective-permute-start(bf16[256,2048]{1,0:T(8,128)(2,1)} %param.11), channel_id=1, source_target_pairs={{0,1},{1,0},{2,3},{3,2},{4,5},{5,4},{6,7},{7,6},{8,9},{9,8},{10,11... | collective-permute-start | bytes 3145736 | tf_op jit(solution)/shard_map/ppermute | solution.py:59
  135.5 55.1 %collective-permute-start.2 = (bf16[128,2048]{1,0:T(8,128)(2,1)S(1)}, bf16[128,2048]{1,0:T(8,128)(2,1)}, u32[]{:S(2)}, u32[]{:S(2)}) collective-permute-start(bf16[128,2048]{1,0:T(8,128)(2,1)S(1)} %get-tuple-element.17), channel_id=1, source_target_pairs={{0,2},{1,3},{2,4},{3,5},{4,6},{5,7},{6,0},{7,1},{8,10},{9,11},{10,... | collective-permute-start | bytes 1572872 | tf_op jit(solution)/shard_map/ppermute | solution.py:75
  137.1 64.8 %collective-permute-start.3 = (bf16[128,2048]{1,0:T(8,128)(2,1)S(1)}, bf16[128,2048]{1,0:T(8,128)(2,1)}, u32[]{:S(2)}, u32[]{:S(2)}) collective-permute-start(bf16[128,2048]{1,0:T(8,128)(2,1)S(1)} %get-tuple-element.19), channel_id=1, source_target_pairs={{0,4},{1,5},{2,6},{3,7},{4,0},{5,1},{6,2},{7,3},{8,12},{9,13},{10,... | collective-permute-start | bytes 1572872 | tf_op jit(solution)/shard_map/ppermute | solution.py:75
  138.1 66.0 %collective-permute-start.4 = (bf16[128,2048]{1,0:T(8,128)(2,1)S(1)}, bf16[128,2048]{1,0:T(8,128)(2,1)}, u32[]{:S(2)}, u32[]{:S(2)}) collective-permute-start(bf16[128,2048]{1,0:T(8,128)(2,1)S(1)} %get-tuple-element.18), channel_id=1, source_target_pairs={{0,6},{1,7},{2,0},{3,1},{4,2},{5,3},{6,4},{7,5},{8,14},{9,15},{10,... | collective-permute-start | bytes 1572872 | tf_op jit(solution)/shard_map/ppermute | solution.py:75
Sparse Core Ops, SparseCore 0:
  9.6 77.0 all-gather.4
  103.5 54.5 all-gather.6
